TPU v7x, 512 devices: a whole 4x4x16 slice. The times are simulated.
512 devices in a mesh: seg: 64 (over y, z_lo, core), blk: 8 (over x, z_hi).
Axes of the slice: x: 4, y: 4, z: 16 (z_hi: 2, z_lo: 8; z = z_hi * 8 + z_lo), core: 2. Of those that a mesh axis runs over, the one named last changes fastest.
Arguments:
- record: float32 [24, 262144], P(None, ('seg', 'blk')), may hold values from -8 to 8, as said below
- templates: bfloat16 [128, 24, 512], P('blk'), may hold values from -6 to 6
Outputs:
- detection: float32 [128, 262144], P(None, ('seg', 'blk'))
Inputs may be any that keep to these rules, and one draw needn't show every extreme that they name: `record`: network samples.
All inputs are finite; a program needn't handle non-finite values.
Results may differ from a plain program's by a relative error of at most 0.0032.
Values may be sent and summed in bfloat16 or wider, within the bound.
No kernel may reach another device: no remote copies, remote signals or barrier semaphores. Data moves between devices by JAX's collectives and lax.ppermute only.
A program may use at most 64 MiB of HBM per device.

v0:
```python
import jax
import jax.numpy as jnp
from jax import lax
from jax.sharding import PartitionSpec as P


def passed_along(block, axis, distance):
    devices = range(lax.axis_size(axis))
    route = [(i - distance, i) for i in devices if i - distance in devices]
    return lax.ppermute(block, axis, route)


def normalize(templates):
    widened = templates.astype(jnp.float32)
    centred = widened - jnp.mean(widened, axis=2, keepdims=True)
    return (centred / jnp.sqrt(jnp.sum(centred * centred, axis=2, keepdims=True) + 1e-06)).astype(
        jnp.bfloat16
    )


def band_matrix(samples, window):
    span = samples + window - 1
    rows = jnp.arange(span, dtype=jnp.int32)[:, None]
    cols = jnp.arange(samples, dtype=jnp.int32)[None, :]
    inside = jnp.logical_and(rows >= cols, rows < cols + window)
    return inside.astype(jnp.float32)


def window_scale(extended, band, window):
    stacked_rows = jnp.concatenate([extended, extended * extended], axis=0)
    sums = jnp.dot(
        stacked_rows, band, precision=lax.Precision.HIGHEST, preferred_element_type=jnp.float32
    )
    channels = extended.shape[0]
    window_sum = sums[:channels]
    window_sq = sums[channels:]
    spread = window_sq - window_sum * window_sum / window
    return 1.0 / jnp.sqrt(jnp.maximum(spread, 1.0))


def correlate(record_bf, kernel_block, scale):
    members = kernel_block.shape[0]
    channels = kernel_block.shape[1]
    window = kernel_block.shape[2]
    samples = scale.shape[1]
    span = record_bf.shape[1]
    kernels = jnp.transpose(kernel_block, (1, 0, 2))

    def one_channel(total, inputs):
        channel_row, kernel_rows, factor = inputs
        repeated = jnp.tile(channel_row, window + 1)[: window * (span + 1)]
        hankel = repeated.reshape(window, span + 1)[:, :samples]
        product = jnp.dot(kernel_rows, hankel, preferred_element_type=jnp.float32)
        return (total + product * factor[None, :], None)

    total, unused = lax.scan(
        one_channel, jnp.zeros((members, samples), jnp.float32), (record_bf, kernels, scale)
    )
    return total / channels


def body(record, templates):
    samples = record.shape[1]
    window = templates.shape[2]
    trailing = passed_along(record, ("seg", "blk"), -1)
    padded_rec = jnp.concatenate([record, trailing], axis=1)
    normalized = normalize(templates)
    band = band_matrix(samples, window)
    extended = padded_rec[:, : samples + window - 1]
    scale = window_scale(extended, band, window)
    record_bf = extended.astype(jnp.bfloat16)
    collected = lax.all_gather(normalized, "blk", axis=0, tiled=True)
    stacked = correlate(record_bf, collected, scale)
    power_sum = lax.psum(jnp.sum(stacked * stacked, axis=1), ("seg", "blk"))
    record_len = samples * lax.axis_size("seg") * lax.axis_size("blk")
    return stacked / jnp.sqrt(power_sum / record_len + 1e-06)[:, None]


def solution(mesh):
    return jax.shard_map(
        body,
        mesh=mesh,
        in_specs=(P(None, ("seg", "blk")), P("blk", None, None)),
        out_specs=P(None, ("seg", "blk")),
        check_vma=False,
    )
```

profile of v0, /device:TPU:1, one launch (start us, length us, event | category | flops | bytes accessed | tf_op | source)
XLA Modules:
  0.0 357.7 jit_solution(17654023932856735463)
XLA Ops:
  6.5 1.2 convert_reduce_fusion
  7.7 1.3 fusion.11
  9.0 1.9 fusion.12
  11.0 19.0 %collective-permute-start = (f32[24,512]{1,0:T(8,128)}, f32[24,512]{1,0:T(8,128)S(1)}, u32[]{:S(2)}, u32[]{:S(2)}) collective-permute-start(f32[24,512]{1,0:T(8,128)} %param.4), channel_id=1, source_target_pairs={{1,0},{2,1},{3,2},{4,3},{5,4},{6,5},{7,6},{8,7},{9,8},{10,9},{11,1... | collective-permute-start | bytes 147464 | tf_op jit(solution)/shard_map/ppermute | solution.py:10
  30.0 1.5 collective-permute-done
  31.5 0.8 fusion.6
  32.4 129.1 %all-gather.2.cloned.1.call-done = bf16[128,24,512]{2,0,1:T(8,128)(2,1)} async-done(((bf16[16,24,512]{2,0,1:T(8,128)(2,1)}), bf16[128,24,512]{2,0,1:T(8,128)(2,1)}) %all-gather.2.cloned.1.call-update) | async-done | bytes 3145744 | tf_op jit(solution)/shard_map/all_gather | solution.py:72
  161.6 86.4 %while.11 = (s32[]{:T(128)}, f32[128,512]{1,0:T(8,128)S(1)}, bf16[24,128,512]{2,1,0:T(8,128)(2,1)}, bf16[24,1023]{1,0:T(8,128)(2,1)S(1)}, f32[24,512]{1,0:T(8,128)S(1)}, /*index=5*/s32[]{:T(128)}, s32[]{:T(128)}) while((s32[]{:T(128)}, f32[128,512]{1,0:T(8,128)S(1)}, bf16[24,128,512]{2,1,0:T(8,128)(2,1)}, ...), condition=%wide.region_3.4_spmd.clone, body=%wide.region_2.3_spmd.clone.sunk | while | flops 67305472 | bytes 8535635 | solution.py:56
  161.7 1.6 tile.17
  163.4 0.5 reshape.22
  164.0 1.2 fusion.28
  165.3 1.6 tile.17
  167.0 0.5 reshape.22
  167.6 1.2 fusion.28
  168.9 1.6 tile.17
  170.6 0.5 reshape.22
  171.2 1.2 fusion.28
  172.5 1.6 tile.17
  174.2 0.5 reshape.22
  174.8 1.2 fusion.28
  176.1 1.6 tile.17
  178.3 1.2 fusion.28
  179.7 1.6 tile.17
  181.9 1.2 fusion.28
  183.3 1.6 tile.17
  185.5 1.2 fusion.28
  186.9 1.6 tile.17
  189.1 1.2 fusion.28
  190.5 1.6 tile.17
  192.7 1.2 fusion.28
  194.1 1.6 tile.17
  196.3 1.2 fusion.28
  197.7 1.6 tile.17
  199.4 0.5 reshape.22
  199.9 1.2 fusion.28
  201.3 1.6 tile.17
  203.0 0.5 reshape.22
  203.5 1.2 fusion.28
  204.9 1.6 tile.17
  207.1 1.2 fusion.28
  208.5 1.6 tile.17
  210.7 1.2 fusion.28
  212.1 1.6 tile.17
  214.3 1.2 fusion.28
  215.7 1.6 tile.17
  217.9 1.2 fusion.28
  219.3 1.6 tile.17
  221.5 1.2 fusion.28
  222.9 1.6 tile.17
  225.1 1.2 fusion.28
  226.5 1.6 tile.17
  228.7 1.2 fusion.28
  230.1 1.6 tile.17
  232.3 1.2 fusion.28
  233.7 1.6 tile.17
  235.9 1.2 fusion.28
  237.3 1.6 tile.17
  239.5 1.2 fusion.28
  240.9 1.6 tile.17
  243.1 1.2 fusion.28
  244.5 1.6 tile.17
  246.7 1.2 fusion.28
  248.1 102.0 %psum.7 = f32[128]{0:T(128)S(1)} all-reduce(f32[128]{0:T(128)S(1)} %multiply_reduce_fusion), channel_id=1, replica_groups=mesh['seg'=64,'blk'=8] {'seg','blk'}, use_global_device_ids=true, to_apply=%region_5.6 | all-reduce | flops 128 | bytes 1024 | tf_op jit(solution)/shard_map/psum | solution.py:74
  350.0 0.8 multiply_divide_fusion
  (127 shorter events, 14.6 us)
Async XLA Ops:
  6.5 25.0 %copy-start = (f32[24,512]{1,0:T(8,128)S(1)}, f32[24,512]{1,0:T(8,128)}, u32[]{:S(2)}) copy-start(f32[24,512]{1,0:T(8,128)} %param.4) | copy-start | bytes 147460
  6.5 155.0 %all-gather.2.cloned.1.call-start = ((), (), s32[]{:S(2)}) async-start(), calls=%async_computation | async-start | bytes 3538944 | tf_op jit(solution)/shard_map/all_gather | solution.py:72
  11.0 20.5 %collective-permute-start = (f32[24,512]{1,0:T(8,128)}, f32[24,512]{1,0:T(8,128)S(1)}, u32[]{:S(2)}, u32[]{:S(2)}) collective-permute-start(f32[24,512]{1,0:T(8,128)} %param.4), channel_id=1, source_target_pairs={{1,0},{2,1},{3,2},{4,3},{5,4},{6,5},{7,6},{8,7},{9,8},{10,9},{11,1... | collective-permute-start | bytes 147464 | tf_op jit(solution)/shard_map/ppermute | solution.py:10
Sparse Core Ops, SparseCore 0:
  11.1 150.3 all-gather.1
where the time goes:
time: 358 us
  waiting for transfers between devices  131 us (37%)
  blocking collectives  102 us (28%)
  local copies, waits for them, and re-layouts  56.6 us (16%)
  matrix products  29 us (8%)
  starting transfers between devices  19 us (5%)
  between operations  13.5 us (4%)
  other arithmetic  5.36 us (1%)
    all_gather x1, waiting for transfers between devices, body(): collected = lax.all_gather(normalized, 'blk', axis=0, tiled=True)  129 us
    psum x1, blocking collectives, body(): power_sum = lax.psum(jnp.sum(stacked * stacked, axis=1), ('seg', 'blk'))  102 us
    another operation x48, local copies, waits for them, and re-layouts, one_channel(): repeated = jnp.tile(channel_row, window + 1)[:window * (span + 1)]  42.1 us
    dot_general x24, matrix products, one_channel(): product = jnp.dot(kernel_rows, hankel, preferred_element_type=jnp.float32)  28.2 us
    ppermute x1, starting transfers between devices, passed_along(): return lax.ppermute(block, axis, route)  19 us
    reshape x24, local copies, waits for them, and re-layouts, one_channel(): hankel = repeated.reshape(window, span + 1)[:, :samples]  11.8 us
  transfers between devices with their start and end apart: 2, of which 2 were waited for; matrix products, arithmetic and copies ran while one was open for 0% of the time, Pallas kernels for 0%

commit v1 on v0

--- a/solution.py
+++ b/solution.py
@@ -71,7 +71,7 @@
     record_bf = extended.astype(jnp.bfloat16)
     collected = lax.all_gather(normalized, "blk", axis=0, tiled=True)
     stacked = correlate(record_bf, collected, scale)
-    power_sum = lax.psum(jnp.sum(stacked * stacked, axis=1), ("seg", "blk"))
+    power_sum = jnp.sum(lax.all_gather(jnp.sum(stacked * stacked, axis=1), ("seg", "blk")), axis=0)
     record_len = samples * lax.axis_size("seg") * lax.axis_size("blk")
     return stacked / jnp.sqrt(power_sum / record_len + 1e-06)[:, None]
 

time: 358 us -> 2180 us (6.09)
  blocking collectives: 102 us -> 1930 us
    all_gather x0 -> x1, blocking collectives: none -> 1930 us  [body(): lax.all_gather(jnp.sum(stacked * stacked, axis=1), ('seg', 'blk'))]
    psum x1 -> x0, blocking collectives: 102 us -> none  [body(): power_sum = lax.psum(jnp.sum(stacked * stacked, axis=1), ('seg', 'blk'))]
where the time goes in v1:
time: 2180 us
  blocking collectives  1930 us (89%)
  waiting for transfers between devices  131 us (6%)
  local copies, waits for them, and re-layouts  56.6 us (3%)
  matrix products  29 us (1%)
    all_gather x1, blocking collectives, body(): lax.all_gather(jnp.sum(stacked * stacked, axis=1), ('seg', 'blk'))  1930 us
    all_gather x1, waiting for transfers between devices, body(): collected = lax.all_gather(normalized, 'blk', axis=0, tiled=True)  129 us
  transfers between devices with their start and end apart: 2, of which 2 were waited for; matrix products, arithmetic and copies ran while one was open for 0% of the time, Pallas kernels for 0%

profile of v1, /device:TPU:1, one launch (start us, length us, event | category | flops | bytes accessed | tf_op | source)
XLA Modules:
  0.0 2181.4 jit_solution(5423996162603695659)
XLA Ops:
  6.5 1.2 convert_reduce_fusion
  7.7 1.3 fusion.11
  9.0 1.9 fusion.12
  11.0 19.0 collective-permute-start
  30.0 1.5 collective-permute-done
  31.5 0.8 fusion.6
  32.4 129.1 %all-gather.4.cloned.1.call-done = bf16[128,24,512]{2,0,1:T(8,128)(2,1)} async-done(((bf16[16,24,512]{2,0,1:T(8,128)(2,1)}), bf16[128,24,512]{2,0,1:T(8,128)(2,1)}) %all-gather.4.cloned.1.call-update) | async-done | bytes 3145744 | tf_op jit(solution)/shard_map/all_gather | solution.py:72
  161.6 86.4 %while.11 = (s32[]{:T(128)}, f32[128,512]{1,0:T(8,128)S(1)}, bf16[24,128,512]{2,1,0:T(8,128)(2,1)}, bf16[24,1023]{1,0:T(8,128)(2,1)S(1)}, f32[24,512]{1,0:T(8,128)S(1)}, /*index=5*/s32[]{:T(128)}, s32[]{:T(128)}) while((s32[]{:T(128)}, f32[128,512]{1,0:T(8,128)S(1)}, bf16[24,128,512]{2,1,0:T(8,128)(2,1)}, ...), condition=%wide.region_3.4_spmd.clone, body=%wide.region_2.3_spmd.clone.sunk | while | flops 67305472 | bytes 8535635 | solution.py:56
  161.7 1.6 tile.17
  163.4 0.5 reshape.30
  164.0 1.2 fusion.28
  165.3 1.6 tile.17
  167.0 0.5 reshape.30
  167.6 1.2 fusion.28
  168.9 1.6 tile.17
  170.6 0.5 reshape.30
  171.2 1.2 fusion.28
  172.5 1.6 tile.17
  174.8 1.2 fusion.28
  176.1 1.6 tile.17
  178.3 1.2 fusion.28
  179.7 1.6 tile.17
  181.9 1.2 fusion.28
  183.3 1.6 tile.17
  185.5 1.2 fusion.28
  186.9 1.6 tile.17
  189.1 1.2 fusion.28
  190.5 1.6 tile.17
  192.7 1.2 fusion.28
  194.1 1.6 tile.17
  196.3 1.2 fusion.28
  197.7 1.6 tile.17
  199.4 0.5 reshape.30
  199.9 1.2 fusion.28
  201.3 1.6 tile.17
  203.0 0.5 reshape.30
  203.5 1.2 fusion.28
  204.9 1.6 tile.17
  207.1 1.2 fusion.28
  208.5 1.6 tile.17
  210.7 1.2 fusion.28
  212.1 1.6 tile.17
  214.3 1.2 fusion.28
  215.7 1.6 tile.17
  217.9 1.2 fusion.28
  219.3 1.6 tile.17
  221.5 1.2 fusion.28
  222.9 1.6 tile.17
  225.1 1.2 fusion.28
  226.5 1.6 tile.17
  228.7 1.2 fusion.28
  230.1 1.6 tile.17
  232.3 1.2 fusion.28
  233.7 1.6 tile.17
  235.9 1.2 fusion.28
  237.3 1.6 tile.17
  239.5 1.2 fusion.28
  240.9 1.6 tile.17
  243.1 1.2 fusion.28
  244.5 1.6 tile.17
  246.7 1.2 fusion.28
  248.1 1925.1 %all-gather.1 = f32[512,1,128]{2,1,0:T(1,128)S(1)} all-gather(f32[1,1,128]{2,1,0:T(1,128)S(1)} %bitcast.12), channel_id=2, replica_groups=mesh['seg'=64,'blk'=8] {'seg','blk'}, dimensions={0}, use_global_device_ids=true | all-gather | bytes 262656 | tf_op jit(solution)/shard_map/all_gather | solution.py:74
  2173.1 0.6 reduce_sum.39
  2173.7 0.8 multiply_divide_fusion
  (128 shorter events, 15.1 us)
Async XLA Ops:
  6.5 25.0 %copy-start = (f32[24,512]{1,0:T(8,128)S(1)}, f32[24,512]{1,0:T(8,128)}, u32[]{:S(2)}) copy-start(f32[24,512]{1,0:T(8,128)} %param.4) | copy-start | bytes 147460
  6.5 155.0 %all-gather.4.cloned.1.call-start = ((), (), s32[]{:S(2)}) async-start(), calls=%async_computation | async-start | bytes 3538944 | tf_op jit(solution)/shard_map/all_gather | solution.py:72
  11.0 20.5 collective-permute-start
Sparse Core Ops, SparseCore 0:
  11.1 150.3 all-gather.3
